TPU v7x, 128 devices: a whole 4x4x4 slice. The times are simulated.
128 devices in a mesh: req: 16 (over z, x), head: 8 (over y, core).
Axes of the slice: x: 4, y: 4, z: 4, core: 2. Of those that a mesh axis runs over, the one named last changes fastest.
Arguments:
- tokens: bfloat16 [256, 1280], P('req'), may hold values from -6 to 6
- w_qkv: bfloat16 [2, 3, 1280, 1280], P(None, None, 'head'), may hold values from -0.15625 to 0.15625
- w_out: bfloat16 [2, 1280, 1280], P(None, 'head'), may hold values from -0.15625 to 0.15625
- w_up: bfloat16 [2, 1280, 1280], P(None, 'head'), may hold values from -0.15625 to 0.15625
- w_down: bfloat16 [2, 1280, 1280], P(None, 'head'), may hold values from -0.15625 to 0.15625
- gain_attn: float32 [2, 1280], replicated, may hold values from 0.1 to 1.9
- gain_mlp: float32 [2, 1280], replicated, may hold values from 0.1 to 1.9
- suffix_cache: bfloat16 [2, 2, 512, 1280, 128], P(None, None, 'req', 'head'), may hold values from -110 to 110
- prompt_cache: bfloat16 [2, 2, 96, 1280, 128], P(None, None, 'req', 'head'), may hold values from -110 to 110
- suffix_table: int32 [16, 32], P('req'), may hold values from 0 to 31, each once within a row
- prompt_owner: int32 [96], replicated, may hold values from 0 to 95, each once
- suffix_len: int32 [256], P('req'), may hold values from 1 to 256, 32768 in all
- group_id: int32 [256], P('req'), may hold values from 0 to 23, never falling along the last dimension, each value on 1 to 16 neighbouring positions
Outputs:
- hidden: bfloat16 [256, 1280], P('req')
- new_cache: bfloat16 [2, 2, 256, 1280], P(None, None, 'req', 'head')
Inputs may be any that keep to these rules, and one draw needn't show every extreme that they name: `suffix_table`: each row holds every number once. `prompt_owner`: each number once. `group_id`: never falls from one request to the next; every group has 1 to 16 requests, one group exactly 16.
All inputs are finite; a program needn't handle non-finite values. No bound on the sum of `suffix_len` on one device may be relied on, other than what follows from the above.
Results may differ from a plain program's by a relative error of at most 0.019.
The roundings to bfloat16 on the way count: a program that leaves them out, or rounds other values in their place, can miss the bound.
Values may be sent and summed in bfloat16 or wider, within the bound.
No kernel may reach another device: no remote copies, remote signals or barrier semaphores. Data moves between devices by JAX's collectives and lax.ppermute only.
A program may use at most 128 MiB of HBM per device.

v0:
```python
import math
import jax
import jax.numpy as jnp
from jax import lax
from jax.sharding import PartitionSpec as P

HD = 80
PPAGES = 4
NEG_FLOOR = -1e30


def root_norm(values, gains):
    factor = lax.rsqrt(jnp.mean(values * values, axis=-1, keepdims=True) + 1e-06)
    return values * factor * gains


def page_groups(prompt_owner, count, page_len):
    owners = prompt_owner // PPAGES
    return jnp.repeat(owners, page_len, total_repeat_length=count * page_len)


def attend(
    query, key_new, val_new, layer_suffix, layer_prompt, pages, valid, group_id, prompt_owner
):
    row_count = query.shape[0]
    head_count = query.shape[1] // HD
    scale = 1.0 / math.sqrt(HD)
    page_len = layer_suffix.shape[3]
    own_pages = pages.shape[1]
    query_heads = query.reshape(row_count, head_count, HD)
    key_heads = key_new.reshape(row_count, head_count, HD)
    val_heads = val_new.reshape(row_count, head_count, HD)
    gathered_pages = layer_suffix[:, pages].reshape(
        2, row_count, own_pages, head_count, HD, page_len
    )
    scores = (
        jnp.einsum(
            "rhd,rphdt->rhpt", query_heads, gathered_pages[0], preferred_element_type=jnp.float32
        ).reshape(row_count, head_count, own_pages * page_len)
        * scale
    )
    own = (
        jnp.einsum("rhd,rhd->rh", query_heads, key_heads, preferred_element_type=jnp.float32)
        * scale
    )
    mask = valid[:, None, :]
    local_top = jnp.maximum(jnp.max(jnp.where(mask, scores, NEG_FLOOR), axis=-1), own)
    weights = jnp.exp(jnp.where(mask, scores - local_top[..., None], NEG_FLOOR))
    own_weight = jnp.exp(own - local_top)
    total = jnp.sum(weights, axis=-1) + own_weight
    weight_pages = weights.astype(jnp.bfloat16).reshape(row_count, head_count, own_pages, page_len)
    mixed = jnp.einsum(
        "rhpt,rphdt->rhd", weight_pages, gathered_pages[1], preferred_element_type=jnp.float32
    )
    mixed = mixed + jnp.einsum(
        "rh,rhd->rhd",
        own_weight.astype(jnp.bfloat16),
        val_heads,
        preferred_element_type=jnp.float32,
    )
    piece = lax.all_gather(layer_prompt, "req", axis=1, tiled=True)
    count = piece.shape[1]
    key_group = page_groups(prompt_owner, count, page_len)
    keys = piece[0].reshape(count, head_count, HD, page_len)
    vals = piece[1].reshape(count, head_count, HD, page_len)
    block = (
        jnp.einsum("rhd,phdt->rhpt", query_heads, keys, preferred_element_type=jnp.float32).reshape(
            row_count, head_count, count * page_len
        )
        * scale
    )
    match = (group_id[:, None] == key_group[None, :])[:, None, :]
    new_top = jnp.maximum(local_top, jnp.max(jnp.where(match, block, NEG_FLOOR), axis=-1))
    block_weights = jnp.exp(jnp.where(match, block - new_top[..., None], NEG_FLOOR))
    factor = jnp.exp(local_top - new_top)
    new_total = total * factor + jnp.sum(block_weights, axis=-1)
    block_rounded = block_weights.astype(jnp.bfloat16).reshape(
        row_count, head_count, count, page_len
    )
    new_mixed = mixed * factor[..., None] + jnp.einsum(
        "rhpt,phdt->rhd", block_rounded, vals, preferred_element_type=jnp.float32
    )
    return (new_mixed / new_total[..., None]).reshape(row_count, -1).astype(jnp.bfloat16)


def add_branch(residual, partial_value, gains, closing):
    residual = residual + lax.psum(partial_value, "head")
    if closing:
        normed = None
    else:
        normed = root_norm(residual, gains).astype(jnp.bfloat16)
    return (residual, normed)


def local(
    tokens,
    w_qkv,
    w_out,
    w_up,
    w_down,
    gain_attn,
    gain_mlp,
    suffix_cache,
    prompt_cache,
    suffix_table,
    prompt_owner,
    suffix_len,
    group_id,
):
    row_count = tokens.shape[0]
    layer_count = w_qkv.shape[0]
    width_here = w_qkv.shape[2]
    model_width = w_qkv.shape[3]
    pages = suffix_table[0].reshape(row_count, -1)
    span = pages.shape[1] * suffix_cache.shape[4]
    valid = jnp.arange(span, dtype=jnp.int32)[None, :] < suffix_len[:, None]
    whole = tokens.astype(jnp.float32)
    normed = root_norm(whole, gain_attn[0]).astype(jnp.bfloat16)
    residual = whole
    new_keys = []
    new_vals = []
    for layer in range(layer_count):
        projected = jnp.einsum(
            "rd,kd->rk",
            normed,
            w_qkv[layer].reshape(3 * width_here, model_width),
            preferred_element_type=jnp.float32,
        )
        projected = projected.reshape(row_count, 3, width_here).astype(jnp.bfloat16)
        query = projected[:, 0]
        key_new = projected[:, 1]
        val_new = projected[:, 2]
        new_keys.append(key_new)
        new_vals.append(val_new)
        attended = attend(
            query,
            key_new,
            val_new,
            suffix_cache[layer],
            prompt_cache[layer],
            pages,
            valid,
            group_id,
            prompt_owner,
        )
        partial_value = jnp.dot(attended, w_out[layer], preferred_element_type=jnp.float32)
        residual, normed = add_branch(residual, partial_value, gain_mlp[layer], False)
        hidden_units = jax.nn.silu(
            jnp.einsum("rd,fd->rf", normed, w_up[layer], preferred_element_type=jnp.float32)
        ).astype(jnp.bfloat16)
        partial_value = jnp.dot(hidden_units, w_down[layer], preferred_element_type=jnp.float32)
        closing = layer == layer_count - 1
        next_gains = gain_attn[layer] if closing else gain_attn[layer + 1]
        residual, normed = add_branch(residual, partial_value, next_gains, closing)
    hidden = residual.astype(jnp.bfloat16)
    new_cache = jnp.stack([jnp.stack(new_keys), jnp.stack(new_vals)], axis=1)
    return (hidden, new_cache)


def solution(mesh):
    placed = (
        P("req", None),
        P(None, None, "head", None),
        P(None, "head", None),
        P(None, "head", None),
        P(None, "head", None),
        P(),
        P(),
        P(None, None, "req", "head", None),
        P(None, None, "req", "head", None),
        P("req", None),
        P(),
        P("req"),
        P("req"),
    )
    return jax.shard_map(
        local,
        mesh=mesh,
        in_specs=placed,
        out_specs=(P("req", None), P(None, None, "req", "head")),
        check_vma=False,
    )
```

profile of v0, /device:TPU:1, one launch (start us, length us, event | category | flops | bytes accessed | tf_op | source)
XLA Modules:
  0.0 431.9 jit_solution(11187171101283764259)
XLA Ops:
  7.3 2.4 fusion.147
  9.7 0.0 all-reduce.5.cloned.1.call-start
  9.8 0.1 fusion.94
  9.9 0.5 fusion.38
  10.4 0.1 reshape_squeeze.31
  10.5 0.1 reshape.287
  10.6 0.1 reshape_squeeze.33
  10.7 0.1 fusion.125
  10.8 0.1 copy.53
  10.8 0.5 broadcast.282
  11.4 0.7 reduce.26
  12.0 0.1 reshape_squeeze.32
  12.1 0.1 reshape.237
  12.2 0.1 reshape.225
  12.3 73.0 %gather_fusion.2 = s32[12288]{0:T(1024)S(1)} fusion(s32[96]{0:T(128)S(1)} %and_select_fusion, s32[12288]{0:T(1024)S(1)} %fusion.97), kind=kCustom, calls=%fused_computation.clone | custom fusion | bytes 147456 | tf_op jit(solution)/shard_map/jit(_take)/gather | solution.py:19
  85.4 4.6 %slice_bitcast_fusion = (bf16[2,32,160,128]{3,2,1,0:T(8,128)(2,1)S(1)}, bf16[2,32,160,128]{3,2,1,0:T(8,128)(2,1)}) fusion(bf16[2,2,32,160,128]{4,3,2,1,0:T(8,128)(2,1)} %param.26), kind=kLoop, calls=%fused_computation.11 | loop fusion | bytes 10485760 | tf_op jit(solution)/shard_map/squeeze | solution.py:139
  90.0 4.1 gather_fusion
  94.2 0.1 broadcast_compare_fusion.1
  94.2 1.9 fusion.146
  96.1 0.3 fusion.26
  96.4 0.1 select_reduce_fusion.1
  96.5 0.2 fusion.116
  96.7 0.2 broadcast_compare_fusion
  96.9 0.4 fusion.24
  97.3 3.6 fusion.144
  101.0 0.8 fusion.11
  101.7 0.5 fusion.28
  102.3 1.2 fusion.62
  103.5 0.1 convert_element_type.71
  103.6 1.8 fusion.86
  105.5 0.7 all-gather.7.cloned.1.call-update
  106.3 2.4 gather_fusion.1
  108.8 3.0 fusion.145
  111.8 53.2 %all-reduce.5.cloned.1.call-done = f32[16,1280]{1,0:T(8,128)} async-done(((f32[16,1280]{1,0:T(8,128)}), f32[16,1280]{1,0:T(8,128)}) %all-reduce.5.cloned.1.call-update) | async-done | bytes 81936 | tf_op jit(solution)/shard_map/psum | solution.py:87
  165.0 1.0 multiply_reduce_fusion.2
  166.1 2.2 fusion.82
  168.3 0.0 all-reduce.9.cloned.1.call-start
  168.3 67.2 %all-gather.7.cloned.1.call-done = bf16[1,2,96,160,128]{4,3,2,1,0:T(8,128)(2,1)} async-done(((bf16[1,2,6,160,128]{4,3,2,1,0:T(8,128)(2,1)}), bf16[1,2,96,160,128]{4,3,2,1,0:T(8,128)(2,1)}) %all-gather.7.cloned.1.call-update) | async-done | bytes 7864336 | tf_op jit(solution)/shard_map/all_gather | solution.py:61
  235.5 5.4 %fusion.143 = (bf16[1,1,96,160,128]{4,3,2,1,0:T(8,128)(2,1)}, bf16[1,1,96,160,128]{4,3,2,1,0:T(8,128)(2,1)}) fusion(bf16[1,2,96,160,128]{4,3,2,1,0:T(8,128)(2,1)} %all-gather.7.cloned.1.call-done), kind=kLoop, calls=%fused_computation.177 | loop fusion | bytes 15728640 | tf_op jit(solution)/shard_map/slice | solution.py:64
  241.0 52.7 %all-reduce.7.cloned.1.call-done = f32[16,1280]{1,0:T(8,128)} async-done(((f32[16,1280]{1,0:T(8,128)}), f32[16,1280]{1,0:T(8,128)}) %all-reduce.7.cloned.1.call-update) | async-done | bytes 81936 | tf_op jit(solution)/shard_map/psum | solution.py:87
  293.7 1.0 multiply_reduce_fusion.1
  294.7 1.7 fusion.41
  296.4 0.1 reshape_squeeze.36
  296.6 0.1 reshape.289
  296.6 0.1 reshape_squeeze.37
  296.7 0.1 fusion.123
  296.8 0.1 copy.66
  296.9 0.3 fusion.22
  297.2 0.1 select_reduce_fusion
  297.3 0.2 fusion.118
  297.5 2.9 fusion.8
  300.3 0.1 reshape.226
  300.4 1.7 fusion.20
  302.2 0.6 fusion.30
  302.7 3.3 fusion.65
  306.1 0.1 convert_element_type.80
  306.2 1.8 fusion.80
  308.0 0.0 all-reduce.11.cloned.1.call-start
  308.1 56.1 %all-reduce.9.cloned.1.call-done = f32[16,1280]{1,0:T(8,128)} async-done(((f32[16,1280]{1,0:T(8,128)}), f32[16,1280]{1,0:T(8,128)}) %all-reduce.9.cloned.1.call-update) | async-done | bytes 81936 | tf_op jit(solution)/shard_map/psum | solution.py:87
  364.2 1.0 multiply_reduce_fusion
  365.2 2.2 fusion.76
  367.4 0.6 copy.45
  368.0 55.5 %all-reduce.11.cloned.1.call-done = f32[16,1280]{1,0:T(8,128)} async-done(((f32[16,1280]{1,0:T(8,128)}), f32[16,1280]{1,0:T(8,128)}) %all-reduce.11.cloned.1.call-update) | async-done | bytes 81936 | tf_op jit(solution)/shard_map/psum | solution.py:87
  423.5 1.5 add_convert_fusion
  (53 shorter events, 0.5 us)
Async XLA Ops:
  7.2 2.6 copy-start.4
  7.2 2.6 copy-start.2
  7.2 2.7 copy-start.3
  7.2 4.2 copy-start.8
  7.2 90.1 %all-gather.5.cloned.1.call-start = ((), (), s32[]{:S(2)}) async-start(), calls=%async_computation.4 | async-start | bytes 8355840 | tf_op jit(solution)/shard_map/all_gather | solution.py:61
  9.6 2.7 copy-start.9
  9.7 155.4 %all-reduce.5.cloned.1.call-start = ((), (), s32[]{:S(2)}) async-start(), calls=%async_computation | async-start | bytes 163840 | tf_op jit(solution)/shard_map/psum | solution.py:87
  90.0 4.2 copy-start.7
  94.2 2.5 copy-start.6
  105.5 130.1 %all-gather.7.cloned.1.call-start = ((), (), s32[]{:S(2)}) async-start(), calls=%async_computation.5 | async-start | bytes 8355840 | tf_op jit(solution)/shard_map/all_gather | solution.py:61
  106.2 187.5 %all-reduce.7.cloned.1.call-start = ((), (), s32[]{:S(2)}) async-start(), calls=%async_computation.1 | async-start | bytes 163840 | tf_op jit(solution)/shard_map/psum | solution.py:87
  106.2 2.5 copy-start.5
  108.7 57.3 %copy-start = (bf16[2,160,1280]{2,1,0:T(8,128)(2,1)S(1)}, bf16[2,160,1280]{2,1,0:T(8,128)(2,1)}, u32[]{:S(2)}) copy-start(bf16[2,160,1280]{2,1,0:T(8,128)(2,1)} %param.23) | copy-start | bytes 2457604
  168.3 125.4 %copy-start.1 = (f32[16,1280]{1,0:T(8,128)S(1)}, f32[16,1280]{1,0:T(8,128)}, u32[]{:S(2)}) copy-start(f32[16,1280]{1,0:T(8,128)} %all-reduce.5.cloned.1.call-done) | copy-start | bytes 245764
  168.3 195.9 %all-reduce.9.cloned.1.call-start = ((), (), s32[]{:S(2)}) async-start(), calls=%async_computation.2 | async-start | bytes 163840 | tf_op jit(solution)/shard_map/psum | solution.py:87
  308.0 115.5 %all-reduce.11.cloned.1.call-start = ((), (), s32[]{:S(2)}) async-start(), calls=%async_computation.3 | async-start | bytes 163840 | tf_op jit(solution)/shard_map/psum | solution.py:87
Sparse Core Ops, SparseCore 0:
  10.2 71.6 all-gather.4
  105.6 59.4 all-reduce.4
  167.2 68.3 all-gather.6
  237.7 55.9 all-reduce.6
  308.1 55.9 all-reduce.8
  367.5 55.9 all-reduce.10
where the time goes:
time: 433 us; the launch traced here: 432 us
  waiting for transfers between devices  286 us (66%)
  local copies, waits for them, and re-layouts  103 us (24%)
  matrix products  21.1 us (5%)
  between operations  14.4 us (3%)
  other arithmetic  7.59 us (2%)
    psum x4, waiting for transfers between devices, add_branch(): residual = residual + lax.psum(partial_value, 'head')  218 us
    gather x1, local copies, waits for them, and re-layouts, page_groups(): return jnp.repeat(owners, page_len, total_repeat_length=count * page_len)  73 us
    all_gather x2, waiting for transfers between devices, attend(): piece = lax.all_gather(layer_prompt, 'req', axis=1, tiled=True)  67.2 us
    slice x2, local copies, waits for them, and re-layouts, attend(): keys = piece[0].reshape(count, head_count, HD, page_len)  9.05 us
  transfers between devices with their start and end apart: 6, of which 5 were waited for; matrix products, arithmetic and copies ran while one was open for 24% of the time, Pallas kernels for 0%

commit v1 on v0

--- a/solution.py
+++ b/solution.py
@@ -58,7 +58,9 @@
         val_heads,
         preferred_element_type=jnp.float32,
     )
-    piece = lax.all_gather(layer_prompt, "req", axis=1, tiled=True)
+    piece = jnp.concatenate(
+        lax.all_to_all(jnp.stack([layer_prompt] * lax.axis_size("req")), "req", 0, 0), axis=1
+    )
     count = piece.shape[1]
     key_group = page_groups(prompt_owner, count, page_len)
     keys = piece[0].reshape(count, head_count, HD, page_len)

time: 433 us -> 474 us (1.095)
  blocking collectives: 0 us -> 97.4 us
  waiting for transfers between devices: 286 us -> 213 us
  local copies, waits for them, and re-layouts: 103 us -> 115 us
  starting transfers between devices: 0.24 us -> 5.18 us
    all_to_all x0 -> x1, blocking collectives: none -> 97.4 us  [attend(): lax.all_to_all(jnp.stack([layer_prompt] * lax.axis_size('req')), 'req', 0...]
    all_gather x2 -> x0, waiting for transfers between devices: 67.2 us -> none  [attend(): piece = lax.all_gather(layer_prompt, 'req', axis=1, tiled=True)]
    psum x4, waiting for transfers between devices: 218 us -> 199 us  [add_branch(): residual = residual + lax.psum(partial_value, 'head')]
    all_to_all x0 -> x1, waiting for transfers between devices: none -> 14.6 us  [attend(): lax.all_to_all(jnp.stack([layer_prompt] * lax.axis_size('req')), 'req', 0...]
    all_to_all x0 -> x2, local copies, waits for them, and re-layouts: none -> 12.4 us  [attend(): lax.all_to_all(jnp.stack([layer_prompt] * lax.axis_size('req')), 'req', 0...]
    another operation x0 -> x2, local copies, waits for them, and re-layouts: none -> 6.69 us  [attend(): jnp.stack([layer_prompt] * lax.axis_size('req'))]
    all_to_all x0 -> x1, starting transfers between devices: none -> 4.83 us  [attend(): lax.all_to_all(jnp.stack([layer_prompt] * lax.axis_size('req')), 'req', 0...]
  transfers between devices with their start and end apart: 6 -> 5, of which waited for: 5 -> 5; matrix products, arithmetic and copies ran while one was open for 24% -> 24% of each run, Pallas kernels for 0% -> 0%
where the time goes in v1:
time: 474 us; the launch traced here: 473 us
  waiting for transfers between devices  213 us (45%)
  local copies, waits for them, and re-layouts  115 us (24%)
  blocking collectives  97.4 us (21%)
  matrix products  20.1 us (4%)
  between operations  14.1 us (3%)
  other arithmetic  7.6 us (2%)
  starting transfers between devices  5.18 us (1%)
    psum x4, waiting for transfers between devices, add_branch(): residual = residual + lax.psum(partial_value, 'head')  199 us
    all_to_all x1, blocking collectives, attend(): lax.all_to_all(jnp.stack([layer_prompt] * lax.axis_size('req')), 'req', 0...  97.4 us
    gather x1, local copies, waits for them, and re-layouts, page_groups(): return jnp.repeat(owners, page_len, total_repeat_length=count * page_len)  73 us
    all_to_all x1, waiting for transfers between devices, attend(): lax.all_to_all(jnp.stack([layer_prompt] * lax.axis_size('req')), 'req', 0...  14.6 us
    all_to_all x2, local copies, waits for them, and re-layouts, attend(): lax.all_to_all(jnp.stack([layer_prompt] * lax.axis_size('req')), 'req', 0...  12.4 us
  transfers between devices with their start and end apart: 5, of which 5 were waited for; matrix products, arithmetic and copies ran while one was open for 24% of the time, Pallas kernels for 0%

profile of v1, /device:TPU:1, one launch (start us, length us, event | category | flops | bytes accessed | tf_op | source)
XLA Modules:
  0.0 473.1 jit_solution(3040093771078235490)
XLA Ops:
  7.2 1.2 slice_bitcast_fusion.2
  8.4 1.8 stack.21
  10.2 97.4 %all_to_all.10 = bf16[16,2,6,160,128]{4,3,2,1,0:T(8,128)(2,1)} all-to-all(bf16[16,2,6,160,128]{4,3,2,1,0:T(8,128)(2,1)S(1)} %stack.21), channel_id=1, replica_groups=mesh['req'=16,'head'=8] {'req'}, dimensions={0} | all-to-all | bytes 15728640 | tf_op jit(solution)/shard_map/all_to_all | solution.py:62
  107.6 4.9 %stack.22 = bf16[16,2,6,160,128]{4,3,2,1,0:T(8,128)(2,1)} broadcast(bf16[2,6,160,128]{3,2,1,0:T(8,128)(2,1)S(1)} %get-tuple-element.57), dimensions={1,2,3,4} | broadcast | bytes 8355840 | tf_op jit(solution)/shard_map/stack | solution.py:62
  112.5 4.8 %all-to-all-start.1 = ((bf16[16,2,6,160,128]{4,3,2,1,0:T(8,128)(2,1)}), bf16[16,2,6,160,128]{4,3,2,1,0:T(8,128)(2,1)}, u32[]{:S(2)}, u32[]{:S(2)}) async-start(bf16[16,2,6,160,128]{4,3,2,1,0:T(8,128)(2,1)} %stack.22), calls=%async_computation.1 | async-start | bytes 15728640 | tf_op jit(solution)/shard_map/all_to_all | solution.py:62
  117.5 0.1 fusion.94
  117.6 0.5 fusion.38
  118.1 0.1 reshape_squeeze.31
  118.2 0.1 reshape.297
  118.3 0.1 reshape_squeeze.33
  118.3 0.1 fusion.125
  118.5 0.5 broadcast.284
  119.1 0.7 reduce.26
  119.7 0.1 reshape_squeeze.32
  119.8 0.1 reshape.257
  119.9 0.1 reshape.245
  120.0 4.5 slice_bitcast_fusion
  124.5 4.2 gather_fusion
  128.7 2.4 gather_fusion.1
  131.1 73.0 %gather_fusion.2 = s32[12288]{0:T(1024)S(1)} fusion(s32[96]{0:T(128)S(1)} %and_select_fusion, s32[12288]{0:T(1024)S(1)} %fusion.97), kind=kCustom, calls=%fused_computation.clone | custom fusion | bytes 147456 | tf_op jit(solution)/shard_map/jit(_take)/gather | solution.py:19
  204.2 0.3 fusion.146
  204.6 0.3 fusion.26
  204.9 0.1 select_reduce_fusion.1
  205.0 0.2 fusion.116
  205.2 0.2 broadcast_compare_fusion
  205.4 0.4 fusion.24
  205.8 0.6 copy-done
  206.3 1.3 fusion.145
  207.6 4.6 copy.180
  212.2 0.6 fusion.144
  212.8 0.8 fusion.11
  213.6 0.5 fusion.28
  214.2 1.2 fusion.62
  215.4 0.1 convert_element_type.71
  215.5 0.8 fusion.86
  216.4 14.6 %all-to-all-done.1 = bf16[16,2,6,160,128]{4,3,2,1,0:T(8,128)(2,1)} async-done(((bf16[16,2,6,160,128]{4,3,2,1,0:T(8,128)(2,1)}), bf16[16,2,6,160,128]{4,3,2,1,0:T(8,128)(2,1)}, u32[]{:S(2)}, u32[]{:S(2)}) %all-to-all-start.1) | async-done | bytes 7864352 | tf_op jit(solution)/shard_map/all_to_all | solution.py:62
  231.0 7.8 %copy.179 = bf16[16,2,6,160,128]{4,3,2,0,1:T(8,128)(2,1)} copy(bf16[16,2,6,160,128]{4,3,2,1,0:T(8,128)(2,1)} %all-to-all-done.1) | data formatting | bytes 15728640 | tf_op jit(solution)/shard_map/all_to_all | solution.py:62
  238.8 36.8 %all-reduce.5.cloned.1.call-done = f32[16,1280]{1,0:T(8,128)} async-done(((f32[16,1280]{1,0:T(8,128)}), f32[16,1280]{1,0:T(8,128)}) %all-reduce.5.cloned.1.call-update) | async-done | bytes 81936 | tf_op jit(solution)/shard_map/psum | solution.py:89
  275.7 1.0 multiply_reduce_fusion.2
  276.7 2.2 fusion.82
  278.9 0.2 all-reduce.9.cloned.1.call-start
  279.2 5.5 %fusion.143 = (bf16[1,16,6,160,128]{4,3,2,1,0:T(8,128)(2,1)}, bf16[1,16,6,160,128]{4,3,2,1,0:T(8,128)(2,1)}) fusion(bf16[2,16,6,160,128]{4,3,2,1,0:T(8,128)(2,1)} %bitcast.212), kind=kLoop, calls=%fused_computation.181 | loop fusion | bytes 15728640 | tf_op jit(solution)/shard_map/slice | solution.py:66
  284.7 50.4 %all-reduce.7.cloned.1.call-done = f32[16,1280]{1,0:T(8,128)} async-done(((f32[16,1280]{1,0:T(8,128)}), f32[16,1280]{1,0:T(8,128)}) %all-reduce.7.cloned.1.call-update) | async-done | bytes 81936 | tf_op jit(solution)/shard_map/psum | solution.py:89
  335.1 1.0 multiply_reduce_fusion.1
  336.1 1.7 fusion.41
  337.9 0.1 reshape_squeeze.36
  338.0 0.1 reshape.299
  338.1 0.1 reshape_squeeze.37
  338.2 0.1 fusion.123
  338.4 0.3 fusion.22
  338.6 0.1 select_reduce_fusion
  338.7 0.2 fusion.118
  338.9 2.9 fusion.8
  341.9 1.8 fusion.20
  343.6 0.6 fusion.30
  344.2 3.4 fusion.65
  347.6 0.1 convert_element_type.80
  347.7 1.8 fusion.80
  349.6 56.1 %all-reduce.9.cloned.1.call-done = f32[16,1280]{1,0:T(8,128)} async-done(((f32[16,1280]{1,0:T(8,128)}), f32[16,1280]{1,0:T(8,128)}) %all-reduce.9.cloned.1.call-update) | async-done | bytes 81936 | tf_op jit(solution)/shard_map/psum | solution.py:89
  405.7 1.0 multiply_reduce_fusion
  406.7 2.2 fusion.76
  408.9 0.6 copy.62
  409.5 55.5 %all-reduce.11.cloned.1.call-done = f32[16,1280]{1,0:T(8,128)} async-done(((f32[16,1280]{1,0:T(8,128)}), f32[16,1280]{1,0:T(8,128)}) %all-reduce.11.cloned.1.call-update) | async-done | bytes 81936 | tf_op jit(solution)/shard_map/psum | solution.py:89
  465.0 1.5 add_convert_fusion
  (62 shorter events, 0.9 us)
Async XLA Ops:
  112.5 4.9 %copy-start.8 = (f32[2,1280]{1,0:T(2,128)S(1)}, f32[2,1280]{1,0:T(2,128)}, u32[]{:S(2)}) copy-start(f32[2,1280]{1,0:T(2,128)} %param.24) | copy-start | bytes 30724
  112.5 5.0 %copy-start.6 = (bf16[16,1280]{1,0:T(8,128)(2,1)S(1)}, bf16[16,1280]{1,0:T(8,128)(2,1)}, u32[]{:S(2)}) copy-start(bf16[16,1280]{1,0:T(8,128)(2,1)} %param.19) | copy-start | bytes 122884
  112.5 5.1 %copy-start.7 = (bf16[2,3,160,1280]{3,2,1,0:T(8,128)(2,1)S(1)}, bf16[2,3,160,1280]{3,2,1,0:T(8,128)(2,1)}, u32[]{:S(2)}) copy-start(bf16[2,3,160,1280]{3,2,1,0:T(8,128)(2,1)} %param.20) | copy-start | bytes 7372804
  112.5 118.5 %all-to-all-start.1 = ((bf16[16,2,6,160,128]{4,3,2,1,0:T(8,128)(2,1)}), bf16[16,2,6,160,128]{4,3,2,1,0:T(8,128)(2,1)}, u32[]{:S(2)}, u32[]{:S(2)}) async-start(bf16[16,2,6,160,128]{4,3,2,1,0:T(8,128)(2,1)} %stack.22), calls=%async_computation.1 | async-start | bytes 15728640 | tf_op jit(solution)/shard_map/all_to_all | solution.py:62
  117.3 1.7 copy-start.12
  117.4 158.3 %all-reduce.5.cloned.1.call-start = ((), (), s32[]{:S(2)}) async-start(), calls=%async_computation.2 | async-start | bytes 163840 | tf_op jit(solution)/shard_map/psum | solution.py:89
  128.7 2.4 copy-start.13
  131.1 73.1 %copy-start.11 = (s32[16]{0:T(128)S(1)}, s32[16]{0:T(128)}, u32[]{:S(2)}) copy-start(s32[16]{0:T(128)} %param.30) | copy-start | bytes 196
  131.1 73.2 %copy-start.1 = (bf16[32,2,160,128]{3,2,1,0:T(8,128)(2,1)S(1)}, bf16[32,2,160,128]{3,2,1,0:T(8,128)(2,1)}, u32[]{:S(2)}) copy-start(bf16[32,2,160,128]{3,2,1,0:T(8,128)(2,1)} %gather_fusion) | copy-start | bytes 7864324
  204.2 0.9 copy-start.10
  204.6 1.7 copy-start
  214.1 1.4 copy-start.4
  214.1 2.2 copy-start.9
  216.3 118.8 %all-reduce.7.cloned.1.call-start = ((), (), s32[]{:S(2)}) async-start(), calls=%async_computation.3 | async-start | bytes 163840 | tf_op jit(solution)/shard_map/psum | solution.py:89
  216.4 60.3 %copy-start.2 = (bf16[2,160,1280]{2,1,0:T(8,128)(2,1)S(1)}, bf16[2,160,1280]{2,1,0:T(8,128)(2,1)}, u32[]{:S(2)}) copy-start(bf16[2,160,1280]{2,1,0:T(8,128)(2,1)} %param.23) | copy-start | bytes 2457604
  278.9 126.7 %all-reduce.9.cloned.1.call-start = ((), (), s32[]{:S(2)}) async-start(), calls=%async_computation.4 | async-start | bytes 163840 | tf_op jit(solution)/shard_map/psum | solution.py:89
  279.2 55.9 %copy-start.5 = (f32[16,1280]{1,0:T(8,128)S(1)}, f32[16,1280]{1,0:T(8,128)}, u32[]{:S(2)}) copy-start(f32[16,1280]{1,0:T(8,128)} %all-reduce.5.cloned.1.call-done) | copy-start | bytes 245764
  344.2 62.5 %copy-start.3 = (bf16[2,160,1280]{2,1,0:T(8,128)(2,1)S(1)}, bf16[2,160,1280]{2,1,0:T(8,128)(2,1)}, u32[]{:S(2)}) copy-start(bf16[2,160,1280]{2,1,0:T(8,128)(2,1)} %param.23) | copy-start | bytes 2457604
  349.5 115.5 %all-reduce.11.cloned.1.call-start = ((), (), s32[]{:S(2)}) async-start(), calls=%async_computation.5 | async-start | bytes 163840 | tf_op jit(solution)/shard_map/psum | solution.py:89
Sparse Core Ops, SparseCore 0:
  216.4 59.1 all-reduce.4
  279.1 55.9 all-reduce.6
  349.6 55.9 all-reduce.8
  409.0 55.9 all-reduce.10
